TPU v7x, 128 devices: a whole 4x4x4 slice. The times are simulated.
128 devices in a mesh: rows: 8 (over x, core), sub: 16 (over z, y).
Axes of the slice: x: 4, y: 4, z: 4, core: 2. Of those that a mesh axis runs over, the one named last changes fastest.
Arguments:
- vectors: float32 [262144, 1024], P(('rows', 'sub')), may hold values from -40 to 40
- list_ids: int32 [262144], P(('rows', 'sub')), may hold values from 0 to 1023
- coarse: float32 [1024, 1024], replicated, may hold values from -3 to 3
- rotation: float32 [1024, 1024], replicated, may hold values from -0.1875 to 0.1875
- codewords: float32 [16, 256, 64], P('sub'), may hold values from -6 to 6
Outputs:
- codebook: float32 [16, 256, 64], P('sub')
- distortion: float32 [16, 262144], P('sub', 'rows')
All inputs are finite; a program needn't handle non-finite values.
Results may differ from a plain program's by a relative error of at most 0.0003.
Values sent between devices are 32-bit elements; how exact they have to be, the bound alone decides.
No kernel may reach another device: no remote copies, remote signals or barrier semaphores. Data moves between devices by JAX's collectives and lax.ppermute only.
A program may use at most 128 MiB of HBM per device.

v0:
```python
import math

import jax
import jax.numpy as jnp
from jax import lax
from jax.sharding import PartitionSpec as P

ITERS = 3


smoothing_factor = 16.0
pseudo_count = 1.0


def soft_stats(drawn_vectors_batch, codebook, requested_sums):
    row_count, sub_width = drawn_vectors_batch.shape
    block_rows = math.gcd(row_count, 2048)
    row_blocks = drawn_vectors_batch.reshape(row_count // block_rows, block_rows, sub_width)
    centroid_lengths = jnp.sum(codebook * codebook, axis=1)

    def accumulate(totals, row_block):
        products = jnp.dot(row_block, codebook.T, precision=lax.Precision.HIGHEST)
        quadratic_error = (
            jnp.sum(row_block * row_block, axis=1, keepdims=True)
            - 2.0 * products
            + centroid_lengths[None, :]
        )
        cluster_affinity_scores = -quadratic_error / smoothing_factor
        row_max = jnp.max(cluster_affinity_scores, axis=1, keepdims=True)
        unnormed = jnp.exp(cluster_affinity_scores - row_max)
        weights = unnormed / jnp.sum(unnormed, axis=1, keepdims=True)
        if requested_sums:
            membership_scaled = totals[0] + jnp.dot(
                weights.T, row_block, precision=lax.Precision.HIGHEST
            )
            masses = totals[1] + jnp.sum(weights, axis=0)
            return ((membership_scaled, masses), None)
        return (totals, jnp.sum(weights * quadratic_error, axis=1) / sub_width)

    start_sums = (
        jnp.zeros(codebook.shape, jnp.float32),
        jnp.zeros((codebook.shape[0],), jnp.float32),
    )
    totals, per_row = lax.scan(accumulate, start_sums, row_blocks)
    if requested_sums:
        return totals
    return per_row.reshape(row_count)


def refit_codebook_entries(codebook, membership_scaled, masses):
    return (membership_scaled + pseudo_count * codebook) / (masses[..., None] + pseudo_count)


def all_stats(drawn_vectors_batch, codebook):
    return lax.map(
        lambda operands: soft_stats(operands[0], operands[1], True), (drawn_vectors_batch, codebook)
    )


def all_distortion(drawn_vectors_batch, codebook):
    return lax.map(
        lambda operands: soft_stats(operands[0], operands[1], False),
        (drawn_vectors_batch, codebook),
    )


def per_device(vectors, list_ids, coarse, rotation, codewords):
    residual = vectors - jnp.take(coarse, list_ids, axis=0)
    rotated = jnp.dot(residual, rotation, precision=lax.Precision.HIGHEST)
    sub_count = codewords.shape[0]
    sub_width = codewords.shape[2]
    owned = lax.all_to_all(rotated, "sub", split_axis=1, concat_axis=0, tiled=True)
    drawn_vectors_batch = jnp.transpose(
        owned.reshape(owned.shape[0], sub_count, sub_width), (1, 0, 2)
    )
    codebook = codewords
    for iteration in range(ITERS):
        membership_scaled, masses = all_stats(drawn_vectors_batch, codebook)
        membership_scaled, masses = lax.psum((membership_scaled, masses), "rows")
        codebook = refit_codebook_entries(codebook, membership_scaled, masses)
    distortion = all_distortion(drawn_vectors_batch, codebook)
    return (codebook, distortion)


def solution(mesh):
    in_specs = (P(("rows", "sub"), None), P(("rows", "sub")), P(), P(), P("sub", None, None))
    out_specs = (P("sub", None, None), P("sub", "rows"))
    return jax.shard_map(
        per_device, mesh=mesh, in_specs=in_specs, out_specs=out_specs, check_vma=False
    )
```

profile of v0, /device:TPU:1, one launch (start us, length us, event | category | flops | bytes accessed | tf_op | source)
XLA Modules:
  0.0 955.3 jit_solution(14642016913725710765)
XLA Ops:
  8.6 14.0 %gather_fusion = f32[2048,1024]{1,0:T(8,128)} fusion(f32[1024,1024]{1,0:T(8,128)} %param.15, s32[2048]{0:T(1024)S(1)} %fusion.58), kind=kCustom, calls=%fused_computation | custom fusion | bytes 16785408 | tf_op jit(solution)/shard_map/jit(_take)/gather | solution.py:68
  22.5 33.9 %fusion.53 = f32[2048,1024]{0,1:T(8,128)} fusion(f32[1024,1024]{1,0:T(8,128)} %param.16, f32[2048,1024]{1,0:T(8,128)} %param.13, f32[2048,1024]{1,0:T(8,128)} %gather_fusion, pred[2048]{0:T(1024)(128)(4,1)S(1)} %compare_and_fusion), kind=kOutput, calls=%fused_computation.72 | convolution fusion | flops 25773998080 | bytes 29362176 | tf_op jit(solution)/shard_map/dot_general | solution.py:69
  56.4 8.8 all-to-all-start
  65.7 122.8 %all-to-all-done = f32[2048,16,64]{0,2,1:T(8,128)} async-done(((f32[2048,16,64]{0,2,1:T(8,128)}), f32[2048,16,64]{0,2,1:T(8,128)}, u32[]{:S(2)}, u32[]{:S(2)}) %all-to-all-start) | async-done | bytes 8388640 | tf_op jit(solution)/shard_map/all_to_all | solution.py:72
  188.6 12.2 %copy.16 = f32[16,2048,64]{2,1,0:T(8,128)} copy(f32[16,2048,64]{1,2,0:T(8,128)} %bitcast.3) | data formatting | bytes 16777216
  200.8 144.8 %while.84 = (s32[]{:T(128)}, f32[256,64]{0,1:T(8,128)S(1)}, f32[256]{0:T(256)S(1)}, f32[16,2048,64]{2,1,0:T(8,128)}, f32[256,64]{1,0:T(8,128)S(1)}, /*index=5*/f32[256]{0:T(256)S(1)}, s32[]{:T(128)}, s32[]{:T(128)}) while((s32[]{:T(128)}, f32[256,64]{0,1:T(8,128)S(1)}, f32[256]{0:T(256)S(1)}, f32[16,2048,64]{2,1,0:T(8,128)}, ...), condition=%wide.region_6.7_spmd.clone, body=%wide.region_1.6_spmd.clone.sunk | while | flops 812411136 | bytes 11286628 | solution.py:44
  206.4 3.4 convolution_add_fusion.6
  215.5 3.4 convolution_add_fusion.6
  224.5 3.4 convolution_add_fusion.6
  233.6 3.4 convolution_add_fusion.6
  242.6 3.4 convolution_add_fusion.6
  251.7 3.4 convolution_add_fusion.6
  260.7 3.4 convolution_add_fusion.6
  269.8 3.4 convolution_add_fusion.6
  278.8 3.4 convolution_add_fusion.6
  287.9 3.4 convolution_add_fusion.6
  297.0 3.4 convolution_add_fusion.6
  306.0 3.4 convolution_add_fusion.6
  315.1 3.4 convolution_add_fusion.6
  324.1 3.4 convolution_add_fusion.6
  333.2 3.4 convolution_add_fusion.6
  345.6 13.5 %psum.43 = f32[1,256]{1,0:T(1,128)S(1)} all-reduce(f32[1,256]{1,0:T(1,128)S(1)} %bitcast.111), channel_id=1, replica_groups=mesh['rows'=8,'sub'=16] {'rows'}, use_global_device_ids=true, to_apply=%region_8.9 | all-reduce | flops 256 | bytes 2048 | tf_op jit(solution)/shard_map/psum | solution.py:79
  359.3 56.0 %all-reduce.4.cloned.1.call-done = f32[1,256,64]{1,2,0:T(8,128)} async-done(((f32[1,256,64]{1,2,0:T(8,128)}), f32[1,256,64]{1,2,0:T(8,128)}) %all-reduce.4.cloned.1.call-update) | async-done | bytes 65552 | tf_op jit(solution)/shard_map/psum | solution.py:79
  416.2 144.8 %while.85 = (s32[]{:T(128)}, f32[256,64]{0,1:T(8,128)S(1)}, f32[256]{0:T(256)S(1)}, f32[16,2048,64]{2,1,0:T(8,128)}, f32[256,64]{1,0:T(8,128)S(1)}, /*index=5*/f32[256]{0:T(256)S(1)}, s32[]{:T(128)}, s32[]{:T(128)}) while((s32[]{:T(128)}, f32[256,64]{0,1:T(8,128)S(1)}, f32[256]{0:T(256)S(1)}, f32[16,2048,64]{2,1,0:T(8,128)}, ...), condition=%wide.region_15.16_spmd.clone, body=%wide.region_10.15_spmd.clone.sunk | while | flops 812411136 | bytes 11286628 | solution.py:44
  561.0 14.7 %psum.45 = f32[1,256]{1,0:T(1,128)S(1)} all-reduce(f32[1,256]{1,0:T(1,128)S(1)} %bitcast.110), channel_id=1, replica_groups=mesh['rows'=8,'sub'=16] {'rows'}, use_global_device_ids=true, to_apply=%region_17.18 | all-reduce | flops 256 | bytes 2048 | tf_op jit(solution)/shard_map/psum | solution.py:79
  576.1 56.6 %all-reduce.6.cloned.1.call-done = f32[1,256,64]{1,2,0:T(8,128)} async-done(((f32[1,256,64]{1,2,0:T(8,128)}), f32[1,256,64]{1,2,0:T(8,128)}) %all-reduce.6.cloned.1.call-update) | async-done | bytes 65552 | tf_op jit(solution)/shard_map/psum | solution.py:79
  633.7 144.8 %while.86 = (s32[]{:T(128)}, f32[256,64]{0,1:T(8,128)S(1)}, f32[256]{0:T(256)S(1)}, f32[16,2048,64]{2,1,0:T(8,128)}, f32[256,64]{1,0:T(8,128)S(1)}, /*index=5*/f32[256]{0:T(256)S(1)}, s32[]{:T(128)}, s32[]{:T(128)}) while((s32[]{:T(128)}, f32[256,64]{0,1:T(8,128)S(1)}, f32[256]{0:T(256)S(1)}, f32[16,2048,64]{2,1,0:T(8,128)}, ...), condition=%wide.region_24.25_spmd.clone, body=%wide.region_19.24_spmd.clone.sunk | while | flops 812411136 | bytes 11286628 | solution.py:44
  639.4 3.4 convolution_add_fusion.8
  648.4 3.4 convolution_add_fusion.8
  778.6 14.7 %psum.47 = f32[1,256]{1,0:T(1,128)S(1)} all-reduce(f32[1,256]{1,0:T(1,128)S(1)} %bitcast.109), channel_id=1, replica_groups=mesh['rows'=8,'sub'=16] {'rows'}, use_global_device_ids=true, to_apply=%region_26.27 | all-reduce | flops 256 | bytes 2048 | tf_op jit(solution)/shard_map/psum | solution.py:79
  793.3 56.9 %all-reduce.8.cloned.1.call-done = f32[1,256,64]{1,2,0:T(8,128)} async-done(((f32[1,256,64]{1,2,0:T(8,128)}), f32[1,256,64]{1,2,0:T(8,128)}) %all-reduce.8.cloned.1.call-update) | async-done | bytes 65552 | tf_op jit(solution)/shard_map/psum | solution.py:79
  851.7 96.2 %while.83 = (s32[]{:T(128)}, f32[16,2048]{1,0:T(8,128)S(1)}, f32[16,2048,64]{2,1,0:T(8,128)}, f32[256,64]{1,0:T(8,128)S(1)}, f32[256]{0:T(256)S(1)}, /*index=5*/s32[]{:T(128)}, s32[]{:T(128)}) while((s32[]{:T(128)}, f32[16,2048]{1,0:T(8,128)S(1)}, f32[16,2048,64]{2,1,0:T(8,128)}, f32[256,64]{1,0:T(8,128)S(1)}, f32[256]{0:T(256)S(1)}, ...), condition=%wide.region_33.34_spmd, body=%wide.region_28.33_spmd.sunk | while | flops 411297792 | bytes 8029781 | solution.py:44
  (404 shorter events, 477.1 us)
Async XLA Ops:
  56.4 9.1 copy-start
  56.4 132.1 %all-to-all-start = ((f32[2048,16,64]{0,2,1:T(8,128)}), f32[2048,16,64]{0,2,1:T(8,128)}, u32[]{:S(2)}, u32[]{:S(2)}) async-start(f32[2048,16,64]{0,2,1:T(8,128)} %bitcast.98), calls=%async_computation | async-start | bytes 16777216 | tf_op jit(solution)/shard_map/all_to_all | solution.py:72
  65.2 350.0 %all-reduce.4.cloned.1.call-start = ((), (), s32[]{:S(2)}) async-start(), calls=%async_computation.1 | async-start | bytes 131072 | tf_op jit(solution)/shard_map/psum | solution.py:79
  345.6 13.6 %copy-start.4 = (f32[256,64]{0,1:T(8,128)}, f32[256,64]{0,1:T(8,128)S(1)}, u32[]{:S(2)}) copy-start(f32[256,64]{0,1:T(8,128)S(1)} %get-tuple-element.185) | copy-start | bytes 196612
  359.2 273.5 %all-reduce.6.cloned.1.call-start = ((), (), s32[]{:S(2)}) async-start(), calls=%async_computation.2 | async-start | bytes 131072 | tf_op jit(solution)/shard_map/psum | solution.py:79
  561.0 14.8 %copy-start.3 = (f32[256,64]{0,1:T(8,128)}, f32[256,64]{0,1:T(8,128)S(1)}, u32[]{:S(2)}) copy-start(f32[256,64]{0,1:T(8,128)S(1)} %get-tuple-element.187) | copy-start | bytes 196612
  575.8 274.4 %all-reduce.8.cloned.1.call-start = ((), (), s32[]{:S(2)}) async-start(), calls=%async_computation.3 | async-start | bytes 131072 | tf_op jit(solution)/shard_map/psum | solution.py:79
  778.5 14.8 %copy-start.2 = (f32[256,64]{0,1:T(8,128)}, f32[256,64]{0,1:T(8,128)S(1)}, u32[]{:S(2)}) copy-start(f32[256,64]{0,1:T(8,128)S(1)} %get-tuple-element.189) | copy-start | bytes 196612
  851.1 0.6 copy-start.1
Sparse Core Ops, SparseCore 0:
  359.3 55.8 all-reduce.3
  575.9 56.7 all-reduce.5
  793.4 56.7 all-reduce.7
where the time goes:
time: 965 us; the launch traced here: 955 us
  matrix products  409 us (42%)
  waiting for transfers between devices  292 us (30%)
  other arithmetic  154 us (16%)
  blocking collectives  43 us (4%)
  local copies, waits for them, and re-layouts  31.2 us (3%)
  between operations  13.9 us (1%)
    dot_general x64, matrix products, accumulate(): products = jnp.dot(row_block, codebook.T, precision=lax.Precision.HIGHEST)  212 us
    psum x3, waiting for transfers between devices, per_device(): membership_scaled, masses = lax.psum((membership_scaled, masses), 'rows')  169 us
    dot_general x48, matrix products, accumulate(): jnp.dot(weights.T, row_block, precision=lax.Precision.HIGHEST)  162 us
    all_to_all x1, waiting for transfers between devices, per_device(): lax.all_to_all(rotated, 'sub', split_axis=1, concat_axis=0, tiled=True)  123 us
    reduce_sum x64, other arithmetic, accumulate(): jnp.sum(row_block * row_block, axis=1, keepdims=True) - 2.0 * products  100 us
    psum x3, blocking collectives, per_device(): membership_scaled, masses = lax.psum((membership_scaled, masses), 'rows')  43 us
    dot_general x1, matrix products, per_device(): rotated = jnp.dot(residual, rotation, precision=lax.Precision.HIGHEST)  33.9 us
    reduce_sum x48, other arithmetic, accumulate(): masses = totals[1] + jnp.sum(weights, axis=0)  20.8 us
  transfers between devices with their start and end apart: 4, of which 4 were waited for; matrix products, arithmetic and copies ran while one was open for 0% of the time, Pallas kernels for 0%

commit v1 on v0

v1 whole, which is shorter than its diff:
```python
import functools

import jax
import jax.numpy as jnp
from jax import lax
from jax.experimental import pallas as pl
from jax.experimental.pallas import tpu as pltpu
from jax.sharding import PartitionSpec as P

ITERS = 3
BLOCK = 2048

smoothing_factor = 16.0
pseudo_count = 1.0

HI = lax.Precision.HIGHEST


def _scores(c8_ref, bias_ref, xt):
    s = jnp.dot(c8_ref[...], xt, precision=HI, preferred_element_type=jnp.float32)
    return s - bias_ref[...]


def _stats_kernel(c8_ref, bias_ref, xt_ref, acc_ref):
    @pl.when(pl.program_id(0) == 0)
    def _():
        acc_ref[...] = jnp.zeros_like(acc_ref)

    xt = xt_ref[...]
    s = _scores(c8_ref, bias_ref, xt)
    m = jnp.max(s, axis=0, keepdims=True)
    e = jnp.exp(s - m)
    r = 1.0 / jnp.sum(e, axis=0, keepdims=True)
    y = jnp.concatenate([xt * r, jnp.broadcast_to(r, (8, xt.shape[1]))], axis=0)
    acc_ref[...] += lax.dot_general(
        e, y, (((1,), (1,)), ((), ())), precision=HI, preferred_element_type=jnp.float32
    )


def _dist_kernel(c8_ref, bias_ref, xt_ref, out_ref):
    xt = xt_ref[...]
    s = _scores(c8_ref, bias_ref, xt)
    m = jnp.max(s, axis=0, keepdims=True)
    e = jnp.exp(s - m)
    l = jnp.sum(e, axis=0, keepdims=True)
    t = jnp.sum(e * s, axis=0, keepdims=True)
    xx = jnp.sum(xt * xt, axis=0, keepdims=True)
    out_ref[...] = (xx - smoothing_factor * (t / l)) * (1.0 / xt.shape[0])


def _prep(codebook):
    c8 = codebook * 0.125
    bias = jnp.sum(codebook * codebook, axis=1, keepdims=True) * (1.0 / smoothing_factor)
    return c8, bias


def _specs(k, ds):
    return [
        pl.BlockSpec((k, ds), lambda i: (0, 0)),
        pl.BlockSpec((k, 1), lambda i: (0, 0)),
        pl.BlockSpec((ds, BLOCK), lambda i: (0, i)),
    ]


def soft_stats(xt, codebook):
    ds, n = xt.shape
    k = codebook.shape[0]
    c8, bias = _prep(codebook)
    return pl.pallas_call(
        _stats_kernel,
        grid=(n // BLOCK,),
        in_specs=_specs(k, ds),
        out_specs=pl.BlockSpec((k, ds + 8), lambda i: (0, 0)),
        out_shape=jax.ShapeDtypeStruct((k, ds + 8), jnp.float32),
        compiler_params=pltpu.CompilerParams(dimension_semantics=("arbitrary",)),
    )(c8, bias, xt)


def soft_distortion(xt, codebook):
    ds, n = xt.shape
    k = codebook.shape[0]
    c8, bias = _prep(codebook)
    return pl.pallas_call(
        _dist_kernel,
        grid=(n // BLOCK,),
        in_specs=_specs(k, ds),
        out_specs=pl.BlockSpec((1, BLOCK), lambda i: (0, i)),
        out_shape=jax.ShapeDtypeStruct((1, n), jnp.float32),
        compiler_params=pltpu.CompilerParams(dimension_semantics=("arbitrary",)),
    )(c8, bias, xt)


def tree_psum(x, axis, size):
    b = 1
    while b < size:
        x = x + lax.ppermute(x, axis, [(i, i ^ b) for i in range(size)])
        b *= 2
    return x


def per_device(vectors, list_ids, coarse, rotation, codewords, rows_size):
    residual = vectors - jnp.take(coarse, list_ids, axis=0)
    rotated_t = lax.dot_general(
        rotation, residual, (((0,), (1,)), ((), ())), precision=HI
    )
    xt = lax.all_to_all(rotated_t, "sub", split_axis=0, concat_axis=1, tiled=True)
    codebook = codewords[0]
    ds = codebook.shape[1]
    for iteration in range(ITERS):
        acc = soft_stats(xt, codebook)
        acc = tree_psum(acc, "rows", rows_size)
        membership_scaled = acc[:, :ds]
        masses = acc[:, ds]
        codebook = (membership_scaled + pseudo_count * codebook) / (
            masses[:, None] + pseudo_count
        )
    distortion = soft_distortion(xt, codebook)
    return (codebook[None], distortion)


def solution(mesh):
    in_specs = (P(("rows", "sub"), None), P(("rows", "sub")), P(), P(), P("sub", None, None))
    out_specs = (P("sub", None, None), P("sub", "rows"))
    return jax.shard_map(
        functools.partial(per_device, rows_size=mesh.shape["rows"]),
        mesh=mesh,
        in_specs=in_specs,
        out_specs=out_specs,
        check_vma=False,
    )
```

time: 965 us -> 457 us (0.47)
  matrix products: 409 us -> 33.9 us
  Pallas kernels: 0 us -> 216 us
  waiting for transfers between devices: 292 us -> 144 us
  other arithmetic: 154 us -> 8.1 us
  blocking collectives: 43 us -> 0 us
  starting transfers between devices: 9.3 us -> 27.7 us
  between operations: 13.9 us -> 0.71 us
    dot_general x113 -> x1, matrix products: 409 us -> 33.9 us  [per_device(): lax.dot_general(rotation, residual, (((0,), (1,)), ((), ())), precision=HI)]
    pallas_call x0 -> x4, Pallas kernels: none -> 216 us  [the longest x3 178 us: soft_stats(): pl.pallas_call(_stats_kernel, grid=(n // BLOCK,), in_specs=_specs(k, ds),...]
    psum x3 -> x0, waiting for transfers between devices: 169 us -> none  [per_device(): membership_scaled, masses = lax.psum((membership_scaled, masses), 'rows')]
    reduce_sum x196 -> x4, other arithmetic: 152 us -> 1.28 us  [_prep(): jnp.sum(codebook * codebook, axis=1, keepdims=True)]
    psum x3 -> x0, blocking collectives: 43 us -> none  [per_device(): membership_scaled, masses = lax.psum((membership_scaled, masses), 'rows')]
    ppermute x0 -> x9, waiting for transfers between devices: none -> 21.9 us  [tree_psum(): x = x + lax.ppermute(x, axis, [(i, i ^ b) for i in range(size)])]
    ppermute x0 -> x9, starting transfers between devices: none -> 18.9 us  [tree_psum(): x = x + lax.ppermute(x, axis, [(i, i ^ b) for i in range(size)])]
    unnamed x15 -> x4, local copies, waits for them, and re-layouts: 13.8 us -> 0.81 us
  transfers between devices with their start and end apart: 4 -> 10, of which waited for: 4 -> 10; matrix products, arithmetic and copies ran while one was open for 0% -> 0% of each run, Pallas kernels for 0% -> 0%
where the time goes in v1:
time: 457 us; the launch traced here: 456 us
  Pallas kernels  216 us (47%)
  waiting for transfers between devices  144 us (32%)
  matrix products  33.9 us (7%)
  starting transfers between devices  27.7 us (6%)
  local copies, waits for them, and re-layouts  25.7 us (6%)
  other arithmetic  8.1 us (2%)
    pallas_call x3, Pallas kernels, soft_stats(): pl.pallas_call(_stats_kernel, grid=(n // BLOCK,), in_specs=_specs(k, ds),...  178 us
    all_to_all x1, waiting for transfers between devices, per_device(): lax.all_to_all(rotated_t, 'sub', split_axis=0, concat_axis=1, tiled=True)  122 us
    pallas_call x1, Pallas kernels, soft_distortion(): pl.pallas_call(_dist_kernel, grid=(n // BLOCK,), in_specs=_specs(k, ds),...  38.2 us
    dot_general x1, matrix products, per_device(): lax.dot_general(rotation, residual, (((0,), (1,)), ((), ())), precision=HI)  33.9 us
    ppermute x9, waiting for transfers between devices, tree_psum(): x = x + lax.ppermute(x, axis, [(i, i ^ b) for i in range(size)])  21.9 us
    ppermute x9, starting transfers between devices, tree_psum(): x = x + lax.ppermute(x, axis, [(i, i ^ b) for i in range(size)])  18.9 us
    gather x1, local copies, waits for them, and re-layouts, per_device(): residual = vectors - jnp.take(coarse, list_ids, axis=0)  14 us
  transfers between devices with their start and end apart: 10, of which 10 were waited for; matrix products, arithmetic and copies ran while one was open for 0% of the time, Pallas kernels for 0%

profile of v1, /device:TPU:1, one launch (start us, length us, event | category | flops | bytes accessed | tf_op | source)
XLA Modules:
  0.0 456.0 jit_solution(14453600954008200226)
XLA Ops:
  2.0 14.0 %gather_fusion = f32[2048,1024]{1,0:T(8,128)} fusion(f32[1024,1024]{1,0:T(8,128)} %param.7, s32[2048]{0:T(1024)S(1)} %fusion.12), kind=kCustom, calls=%fused_computation | custom fusion | bytes 16785408 | tf_op jit(solution)/shard_map/jit(_take)/gather | solution.py:102
  16.0 33.9 %fusion = f32[2048,1024]{0,1:T(8,128)} fusion(f32[1024,1024]{1,0:T(8,128)} %param.8, f32[2048,1024]{1,0:T(8,128)} %param.5, f32[2048,1024]{1,0:T(8,128)} %gather_fusion, pred[2048]{0:T(1024)(128)(4,1)S(1)} %compare_and_fusion), kind=kOutput, calls=%fused_computation.1 | convolution fusion | flops 25773998080 | bytes 29362176 | tf_op jit(solution)/shard_map/dot_general | solution.py:103
  49.9 8.8 %all-to-all-start = ((f32[16,64,2048]{2,1,0:T(8,128)}), f32[16,64,2048]{2,1,0:T(8,128)}, u32[]{:S(2)}, u32[]{:S(2)}) async-start(f32[16,64,2048]{2,1,0:T(8,128)} %bitcast.23), calls=%async_computation | async-start | bytes 16777216 | tf_op jit(solution)/shard_map/all_to_all | solution.py:106
  60.3 121.8 %all-to-all-done = f32[16,64,2048]{2,1,0:T(8,128)} async-done(((f32[16,64,2048]{2,1,0:T(8,128)}), f32[16,64,2048]{2,1,0:T(8,128)}, u32[]{:S(2)}, u32[]{:S(2)}) %all-to-all-start) | async-done | bytes 8388640 | tf_op jit(solution)/shard_map/all_to_all | solution.py:106
  182.0 7.7 %copy.24 = f32[16,8,8,2048]{3,2,0,1:T(8,128)} copy(f32[16,8,8,2048]{3,2,1,0:T(8,128)} %bitcast.10) | data formatting | bytes 16777216 | tf_op jit(solution)/shard_map/all_to_all | solution.py:106
  189.7 59.3 %shard_map.68 = f32[256,72]{1,0:T(8,128)} custom-call(f32[256,64]{1,0:T(8,128)} %get-tuple-element.15.c8_ref, f32[256,1]{1,0:T(8,128)} %copy.19.bias_ref, f32[64,32768]{1,0:T(8,128)} %bitcast.19), custom_call_target="tpu_custom_call" | custom-call | tf_op jit(solution)/shard_map/pallas_call | solution.py:69
  249.1 1.8 collective-permute-start
  250.8 1.2 collective-permute-done
  252.0 0.9 add.55
  253.0 1.3 collective-permute-start.1
  254.3 3.5 collective-permute-done.1
  257.8 2.8 collective-permute-start.2
  260.6 2.6 collective-permute-done.2
  263.6 0.8 copy.20.bias_ref
  265.0 59.3 %shard_map.69 = f32[256,72]{1,0:T(8,128)} custom-call(f32[256,64]{1,0:T(8,128)} %broadcast_multiply_fusion.2.c8_ref, f32[256,1]{1,0:T(8,128)} %copy.20.bias_ref, f32[64,32768]{1,0:T(8,128)} %bitcast.20), custom_call_target="tpu_custom_call" | custom-call | tf_op jit(solution)/shard_map/pallas_call | solution.py:69
  324.4 2.4 collective-permute-start.3
  326.8 1.2 collective-permute-done.3
  327.9 0.9 add.60
  328.9 1.3 collective-permute-start.4
  330.2 3.5 collective-permute-done.4
  333.7 3.0 collective-permute-start.5
  336.7 2.6 collective-permute-done.5
  339.7 0.8 copy.21.bias_ref
  341.2 59.3 %shard_map.70 = f32[256,72]{1,0:T(8,128)} custom-call(f32[256,64]{1,0:T(8,128)} %broadcast_multiply_fusion.1.c8_ref, f32[256,1]{1,0:T(8,128)} %copy.21.bias_ref, f32[64,32768]{1,0:T(8,128)} %bitcast.21), custom_call_target="tpu_custom_call" | custom-call | tf_op jit(solution)/shard_map/pallas_call | solution.py:69
  400.5 2.4 collective-permute-start.6
  402.9 1.2 collective-permute-done.6
  404.1 0.9 add.65
  405.0 1.3 collective-permute-start.7
  406.3 3.5 collective-permute-done.7
  409.8 2.8 collective-permute-start.8
  412.6 2.6 collective-permute-done.8
  417.8 38.2 %shard_map.71 = f32[1,32768]{1,0:T(1,128)} custom-call(f32[256,64]{1,0:T(8,128)} %broadcast_multiply_fusion.c8_ref, f32[256,1]{1,0:T(8,128)} %copy.22.bias_ref, f32[64,32768]{1,0:T(8,128)} %bitcast.22), custom_call_target="tpu_custom_call" | custom-call | tf_op jit(solution)/shard_map/pallas_call | solution.py:83
  (28 shorter events, 7.7 us)
Async XLA Ops:
  49.9 8.8 %copy-start = (f32[1,256,64]{1,2,0:T(8,128)S(1)}, f32[1,256,64]{1,2,0:T(8,128)}, u32[]{:S(2)}) copy-start(f32[1,256,64]{1,2,0:T(8,128)} %param.9) | copy-start | bytes 196612
  49.9 132.1 %all-to-all-start = ((f32[16,64,2048]{2,1,0:T(8,128)}), f32[16,64,2048]{2,1,0:T(8,128)}, u32[]{:S(2)}, u32[]{:S(2)}) async-start(f32[16,64,2048]{2,1,0:T(8,128)} %bitcast.23), calls=%async_computation | async-start | bytes 16777216 | tf_op jit(solution)/shard_map/all_to_all | solution.py:106
  249.1 3.0 collective-permute-start
  253.0 4.8 %collective-permute-start.1 = (f32[256,72]{1,0:T(8,128)S(1)}, f32[256,72]{1,0:T(8,128)S(1)}, u32[]{:S(2)}, u32[]{:S(2)}) collective-permute-start(f32[256,72]{1,0:T(8,128)S(1)} %add.55), channel_id=1, source_target_pairs={{0,32},{16,48},{32,0},{48,16},{64,96},{80,112},{96,64},{112,80},{1... | collective-permute-start | bytes 221192 | tf_op jit(solution)/shard_map/ppermute | solution.py:96
  257.8 5.4 %collective-permute-start.2 = (f32[256,72]{1,0:T(8,128)S(1)}, f32[256,72]{1,0:T(8,128)S(1)}, u32[]{:S(2)}, u32[]{:S(2)}) collective-permute-start(f32[256,72]{1,0:T(8,128)S(1)} %add.56), channel_id=1, source_target_pairs={{0,64},{16,80},{32,96},{48,112},{64,0},{80,16},{96,32},{112,48},{1... | collective-permute-start | bytes 221192 | tf_op jit(solution)/shard_map/ppermute | solution.py:96
  324.4 3.6 collective-permute-start.3
  328.9 4.8 %collective-permute-start.4 = (f32[256,72]{1,0:T(8,128)S(1)}, f32[256,72]{1,0:T(8,128)S(1)}, u32[]{:S(2)}, u32[]{:S(2)}) collective-permute-start(f32[256,72]{1,0:T(8,128)S(1)} %add.60), channel_id=1, source_target_pairs={{0,32},{16,48},{32,0},{48,16},{64,96},{80,112},{96,64},{112,80},{1... | collective-permute-start | bytes 221192 | tf_op jit(solution)/shard_map/ppermute | solution.py:96
  333.7 5.6 %collective-permute-start.5 = (f32[256,72]{1,0:T(8,128)S(1)}, f32[256,72]{1,0:T(8,128)S(1)}, u32[]{:S(2)}, u32[]{:S(2)}) collective-permute-start(f32[256,72]{1,0:T(8,128)S(1)} %add.61), channel_id=1, source_target_pairs={{0,64},{16,80},{32,96},{48,112},{64,0},{80,16},{96,32},{112,48},{1... | collective-permute-start | bytes 221192 | tf_op jit(solution)/shard_map/ppermute | solution.py:96
  400.5 3.6 collective-permute-start.6
  405.0 4.8 %collective-permute-start.7 = (f32[256,72]{1,0:T(8,128)S(1)}, f32[256,72]{1,0:T(8,128)S(1)}, u32[]{:S(2)}, u32[]{:S(2)}) collective-permute-start(f32[256,72]{1,0:T(8,128)S(1)} %add.65), channel_id=1, source_target_pairs={{0,32},{16,48},{32,0},{48,16},{64,96},{80,112},{96,64},{112,80},{1... | collective-permute-start | bytes 221192 | tf_op jit(solution)/shard_map/ppermute | solution.py:96
  409.8 5.4 %collective-permute-start.8 = (f32[256,72]{1,0:T(8,128)S(1)}, f32[256,72]{1,0:T(8,128)S(1)}, u32[]{:S(2)}, u32[]{:S(2)}) collective-permute-start(f32[256,72]{1,0:T(8,128)S(1)} %add.66), channel_id=1, source_target_pairs={{0,64},{16,80},{32,96},{48,112},{64,0},{80,16},{96,32},{112,48},{1... | collective-permute-start | bytes 221192 | tf_op jit(solution)/shard_map/ppermute | solution.py:96

commit v2 on v1

--- a/solution.py
+++ b/solution.py
@@ -21,6 +21,15 @@
     return s - bias_ref[...]
 
 
+def _split(a):
+    hi = a.astype(jnp.bfloat16)
+    return hi, (a - hi.astype(jnp.float32)).astype(jnp.bfloat16)
+
+
+def _nt(a, b):
+    return lax.dot_general(a, b, (((1,), (1,)), ((), ())), preferred_element_type=jnp.float32)
+
+
 def _stats_kernel(c8_ref, bias_ref, xt_ref, acc_ref):
     @pl.when(pl.program_id(0) == 0)
     def _():
@@ -32,9 +41,9 @@
     e = jnp.exp(s - m)
     r = 1.0 / jnp.sum(e, axis=0, keepdims=True)
     y = jnp.concatenate([xt * r, jnp.broadcast_to(r, (8, xt.shape[1]))], axis=0)
-    acc_ref[...] += lax.dot_general(
-        e, y, (((1,), (1,)), ((), ())), precision=HI, preferred_element_type=jnp.float32
-    )
+    eh, el = _split(e)
+    yh, yl = _split(y)
+    acc_ref[...] += _nt(eh, yh) + _nt(el, yh) + _nt(eh, yl)
 
 
 def _dist_kernel(c8_ref, bias_ref, xt_ref, out_ref):
@@ -90,12 +99,14 @@
     )(c8, bias, xt)
 
 
-def tree_psum(x, axis, size):
-    b = 1
-    while b < size:
-        x = x + lax.ppermute(x, axis, [(i, i ^ b) for i in range(size)])
-        b *= 2
-    return x
+def gathered_psum(x, axis, size):
+    parts = lax.all_to_all(
+        jnp.broadcast_to(x[None], (size,) + x.shape), axis, 0, 0, tiled=True
+    )
+    total = parts[0]
+    for j in range(1, size):
+        total = total + parts[j]
+    return total
 
 
 def per_device(vectors, list_ids, coarse, rotation, codewords, rows_size):
@@ -108,7 +119,7 @@
     ds = codebook.shape[1]
     for iteration in range(ITERS):
         acc = soft_stats(xt, codebook)
-        acc = tree_psum(acc, "rows", rows_size)
+        acc = gathered_psum(acc, "rows", rows_size)
         membership_scaled = acc[:, :ds]
         masses = acc[:, ds]
         codebook = (membership_scaled + pseudo_count * codebook) / (

time: 457 us -> 427 us (0.934)
  blocking collectives: 0 us -> 43.1 us
  Pallas kernels: 216 us -> 182 us
  waiting for transfers between devices: 144 us -> 122 us
  starting transfers between devices: 27.7 us -> 8.78 us
  local copies, waits for them, and re-layouts: 25.7 us -> 31.1 us
    all_to_all x0 -> x3, blocking collectives: none -> 43.1 us  [gathered_psum(): lax.all_to_all(jnp.broadcast_to(x[None], (size,) + x.shape), axis, 0, 0,...]
    pallas_call x3, Pallas kernels: 178 us -> 143 us  [soft_stats(): pl.pallas_call(_stats_kernel, grid=(n // BLOCK,), in_specs=_specs(k, ds),...]
    ppermute x9 -> x0, waiting for transfers between devices: 21.9 us -> none  [tree_psum(): x = x + lax.ppermute(x, axis, [(i, i ^ b) for i in range(size)])]
    ppermute x9 -> x0, starting transfers between devices: 18.9 us -> none  [tree_psum(): x = x + lax.ppermute(x, axis, [(i, i ^ b) for i in range(size)])]
  transfers between devices with their start and end apart: 10 -> 1, of which waited for: 10 -> 1; matrix products, arithmetic and copies ran while one was open for 0% -> 0% of each run, Pallas kernels for 0% -> 0%
where the time goes in v2:
time: 427 us
  Pallas kernels  182 us (43%)
  waiting for transfers between devices  122 us (29%)
  blocking collectives  43.1 us (10%)
  matrix products  33.9 us (8%)
  local copies, waits for them, and re-layouts  31.1 us (7%)
  starting transfers between devices  8.78 us (2%)
  other arithmetic  5.4 us (1%)
    pallas_call x3, Pallas kernels, soft_stats(): pl.pallas_call(_stats_kernel, grid=(n // BLOCK,), in_specs=_specs(k, ds),...  143 us
    all_to_all x1, waiting for transfers between devices, per_device(): lax.all_to_all(rotated_t, 'sub', split_axis=0, concat_axis=1, tiled=True)  122 us
    all_to_all x3, blocking collectives, gathered_psum(): lax.all_to_all(jnp.broadcast_to(x[None], (size,) + x.shape), axis, 0, 0,...  43.1 us
    pallas_call x1, Pallas kernels, soft_distortion(): pl.pallas_call(_dist_kernel, grid=(n // BLOCK,), in_specs=_specs(k, ds),...  38.2 us
    dot_general x1, matrix products, per_device(): lax.dot_general(rotation, residual, (((0,), (1,)), ((), ())), precision=HI)  33.9 us
    gather x1, local copies, waits for them, and re-layouts, per_device(): residual = vectors - jnp.take(coarse, list_ids, axis=0)  14 us
    all_to_all x1, starting transfers between devices, per_device(): lax.all_to_all(rotated_t, 'sub', split_axis=0, concat_axis=1, tiled=True)  8.78 us
  transfers between devices with their start and end apart: 1, of which 1 were waited for; matrix products, arithmetic and copies ran while one was open for 0% of the time, Pallas kernels for 0%

profile of v2, /device:TPU:1, one launch (start us, length us, event | category | flops | bytes accessed | tf_op | source)
XLA Modules:
  0.0 426.6 jit_solution(17636960547228205322)
XLA Ops:
  0.6 0.7 fusion.12
  1.3 0.7 compare_and_fusion
  2.0 14.0 %gather_fusion = f32[2048,1024]{1,0:T(8,128)} fusion(f32[1024,1024]{1,0:T(8,128)} %param.7, s32[2048]{0:T(1024)S(1)} %fusion.12), kind=kCustom, calls=%fused_computation | custom fusion | bytes 16785408 | tf_op jit(solution)/shard_map/jit(_take)/gather | solution.py:113
  16.0 33.9 %fusion = f32[2048,1024]{0,1:T(8,128)} fusion(f32[1024,1024]{1,0:T(8,128)} %param.8, f32[2048,1024]{1,0:T(8,128)} %param.5, f32[2048,1024]{1,0:T(8,128)} %gather_fusion, pred[2048]{0:T(1024)(128)(4,1)S(1)} %compare_and_fusion), kind=kOutput, calls=%fused_computation.1 | convolution fusion | flops 25773998080 | bytes 29362176 | tf_op jit(solution)/shard_map/dot_general | solution.py:114
  49.9 8.8 %all-to-all-start = ((f32[16,64,2048]{2,1,0:T(8,128)}), f32[16,64,2048]{2,1,0:T(8,128)}, u32[]{:S(2)}, u32[]{:S(2)}) async-start(f32[16,64,2048]{2,1,0:T(8,128)} %bitcast.29), calls=%async_computation | async-start | bytes 16777216 | tf_op jit(solution)/shard_map/all_to_all | solution.py:117
  58.8 0.7 fusion.11
  59.5 0.8 copy.19.bias_ref
  60.3 121.8 %all-to-all-done = f32[16,64,2048]{2,1,0:T(8,128)} async-done(((f32[16,64,2048]{2,1,0:T(8,128)}), f32[16,64,2048]{2,1,0:T(8,128)}, u32[]{:S(2)}, u32[]{:S(2)}) %all-to-all-start) | async-done | bytes 8388640 | tf_op jit(solution)/shard_map/all_to_all | solution.py:117
  182.0 7.7 %copy.75 = f32[16,8,8,2048]{3,2,0,1:T(8,128)} copy(f32[16,8,8,2048]{3,2,1,0:T(8,128)} %bitcast.13) | data formatting | bytes 16777216 | tf_op jit(solution)/shard_map/all_to_all | solution.py:117
  189.7 47.8 %shard_map.68 = f32[256,72]{1,0:T(8,128)} custom-call(f32[256,64]{1,0:T(8,128)} %get-tuple-element.39.c8_ref, f32[256,1]{1,0:T(8,128)} %copy.19.bias_ref, f32[64,32768]{1,0:T(8,128)} %bitcast.25), custom_call_target="tpu_custom_call" | custom-call | tf_op jit(solution)/shard_map/pallas_call | solution.py:78
  237.6 1.0 copy.20
  238.6 16.2 %all_to_all.34 = f32[8,256,72]{1,2,0:T(8,128)S(1)} all-to-all(f32[8,256,72]{1,2,0:T(8,128)S(1)} %broadcast_in_dim.40), channel_id=1, replica_groups=mesh['rows'=8,'sub'=16] {'rows'}, dimensions={0} | all-to-all | bytes 1179648 | tf_op jit(solution)/shard_map/all_to_all | solution.py:103
  255.7 0.2 fusion.9
  255.9 0.2 multiply_reduce_fusion.2
  256.1 0.8 copy.29.bias_ref
  256.9 0.7 broadcast_multiply_fusion.2.c8_ref
  257.6 47.8 %shard_map.69 = f32[256,72]{1,0:T(8,128)} custom-call(f32[256,64]{1,0:T(8,128)} %broadcast_multiply_fusion.2.c8_ref, f32[256,1]{1,0:T(8,128)} %copy.29.bias_ref, f32[64,32768]{1,0:T(8,128)} %bitcast.26), custom_call_target="tpu_custom_call" | custom-call | tf_op jit(solution)/shard_map/pallas_call | solution.py:78
  305.4 1.0 copy.30
  306.4 13.4 %all_to_all.35 = f32[8,256,72]{1,2,0:T(8,128)S(1)} all-to-all(f32[8,256,72]{1,2,0:T(8,128)S(1)} %broadcast_in_dim.41), channel_id=1, replica_groups=mesh['rows'=8,'sub'=16] {'rows'}, dimensions={0} | all-to-all | bytes 1179648 | tf_op jit(solution)/shard_map/all_to_all | solution.py:103
  320.8 0.2 fusion.7
  320.9 0.2 multiply_reduce_fusion.1
  321.2 0.8 copy.39.bias_ref
  322.0 0.7 broadcast_multiply_fusion.1.c8_ref
  322.6 47.8 %shard_map.70 = f32[256,72]{1,0:T(8,128)} custom-call(f32[256,64]{1,0:T(8,128)} %broadcast_multiply_fusion.1.c8_ref, f32[256,1]{1,0:T(8,128)} %copy.39.bias_ref, f32[64,32768]{1,0:T(8,128)} %bitcast.27), custom_call_target="tpu_custom_call" | custom-call | tf_op jit(solution)/shard_map/pallas_call | solution.py:78
  370.4 1.0 copy.40
  371.5 13.4 %all_to_all.36 = f32[8,256,72]{1,2,0:T(8,128)S(1)} all-to-all(f32[8,256,72]{1,2,0:T(8,128)S(1)} %broadcast_in_dim.42), channel_id=1, replica_groups=mesh['rows'=8,'sub'=16] {'rows'}, dimensions={0} | all-to-all | bytes 1179648 | tf_op jit(solution)/shard_map/all_to_all | solution.py:103
  385.8 0.2 fusion.5
  386.0 0.2 multiply_reduce_fusion
  386.2 0.8 copy.49.bias_ref
  387.0 0.7 broadcast_multiply_fusion.c8_ref
  387.7 0.7 copy.50
  388.4 38.2 %shard_map.71 = f32[1,32768]{1,0:T(1,128)} custom-call(f32[256,64]{1,0:T(8,128)} %broadcast_multiply_fusion.c8_ref, f32[256,1]{1,0:T(8,128)} %copy.49.bias_ref, f32[64,32768]{1,0:T(8,128)} %bitcast.28), custom_call_target="tpu_custom_call" | custom-call | tf_op jit(solution)/shard_map/pallas_call | solution.py:92
  (40 shorter events, 2.8 us)
Async XLA Ops:
  49.9 8.8 %copy-start = (f32[1,256,64]{1,2,0:T(8,128)S(1)}, f32[1,256,64]{1,2,0:T(8,128)}, u32[]{:S(2)}) copy-start(f32[1,256,64]{1,2,0:T(8,128)} %param.9) | copy-start | bytes 196612
  49.9 132.1 %all-to-all-start = ((f32[16,64,2048]{2,1,0:T(8,128)}), f32[16,64,2048]{2,1,0:T(8,128)}, u32[]{:S(2)}, u32[]{:S(2)}) async-start(f32[16,64,2048]{2,1,0:T(8,128)} %bitcast.29), calls=%async_computation | async-start | bytes 16777216 | tf_op jit(solution)/shard_map/all_to_all | solution.py:117
